TPU v7x, 512 devices: a whole 4x8x8 slice. The times are simulated.
512 devices in a mesh: ctx: 64 (over y_lo, z, core), tp: 8 (over y_hi, x).
Axes of the slice: x: 4, y: 8 (y_hi: 2, y_lo: 4; y = y_hi * 4 + y_lo), z: 8, core: 2. Of those that a mesh axis runs over, the one named last changes fastest.
Arguments:
- tokens: bfloat16 [16384, 2048], P('ctx', 'tp'), may hold values from -6 to 6
- w_in: bfloat16 [2048, 4096], P('ctx', 'tp'), may hold values from -0.125 to 0.125
- w_bc: bfloat16 [2048, 2048], P('ctx', 'tp'), may hold values from -0.01171875 to 0.01171875
- w_dt: bfloat16 [2048, 64], P('ctx', 'tp'), may hold values from -0.125 to 0.125
- dt_bias: float32 [64], P('tp'), may hold values from -2 to 0
- decay_rate: float32 [64], P('tp'), may hold values from 1e-05 to 0.1
- skip_gain: float32 [64], P('tp'), may hold values from 0.5 to 1.5
- w_out: bfloat16 [4096, 2048], P('tp', 'ctx'), may hold values from -0.09375 to 0.09375
- cotangent: bfloat16 [16384, 2048], P('ctx', 'tp'), may hold values from -6 to 6
Outputs:
- output: bfloat16 [16384, 2048], P('ctx', 'tp')
- grad: bfloat16 [16384, 2048], P('ctx', 'tp')
All inputs are finite; a program needn't handle non-finite values.
Results may differ from a plain program's by a relative error of at most 0.0061.
Values may be sent and summed in bfloat16 or wider, within the bound.
No kernel may reach another device: no remote copies, remote signals or barrier semaphores. Data moves between devices by JAX's collectives and lax.ppermute only.
A program may use at most 128 MiB of HBM per device.

v0:
```python
import jax
import jax.numpy as jnp
from jax import lax
from jax.sharding import PartitionSpec as P

HEADDIM = 64
STATE = 128
SPAN = 256
HIGH = lax.Precision.HIGH
RING = 4


def both_carries(decay, forward, backward, axis):
    devices, position = (lax.axis_size(axis), lax.axis_index(axis))
    heads = decay.shape[0]
    own_a = decay[:, None]
    own_s = forward.reshape(heads, -1)
    own_u = backward.reshape(heads, -1)
    size = own_s.shape[1]
    message = jnp.concatenate([own_s, own_u, jnp.broadcast_to(own_a, (heads, 128))], axis=1)
    got = lax.ppermute(message, axis, [(i, i ^ 1) for i in range(devices)])
    sib_s = got[:, :size]
    sib_u = got[:, size : 2 * size]
    sib_a = got[:, 2 * size : 2 * size + 1]
    second = position & 1 != 0
    first_a = jnp.where(second, sib_a, own_a)
    first_s = jnp.where(second, sib_s, own_s)
    last_a = jnp.where(second, own_a, sib_a)
    last_s = jnp.where(second, own_s, sib_s)
    first_u = jnp.where(second, sib_u, own_u)
    last_u = jnp.where(second, own_u, sib_u)
    total_a = first_a * last_a
    total_m = jnp.where(second, first_u + first_a * last_u, last_a * first_s + last_s)
    before_a = jnp.ones_like(total_a)
    before_m = jnp.zeros_like(total_m)
    bit = 2
    while bit < devices:
        if 2 * bit >= devices:
            wanted = [(i, i ^ bit) for i in range(devices) if (i & bit != 0) == (i & 1 != 0)]
            got_m = lax.ppermute(total_m, axis, wanted)
            flag = (position & bit != 0) != second
            before_m = jnp.where(flag, before_a * got_m + before_m, before_m)
            break
        message = jnp.concatenate([total_m, jnp.broadcast_to(total_a, (heads, 128))], axis=1)
        got = lax.ppermute(message, axis, [(i, i ^ bit) for i in range(devices)])
        got_m = got[:, :size]
        got_a = got[:, size : size + 1]
        flag = (position & bit != 0) != second
        before_m = jnp.where(flag, before_a * got_m + before_m, before_m)
        before_a = jnp.where(flag, before_a * got_a, before_a)
        total_m = jnp.where(flag, total_a * got_m + total_m, got_a * total_m + got_m)
        total_a = total_a * got_a
        bit *= 2
    got = lax.ppermute(before_m, axis, [(i, i ^ 1) for i in range(devices)])
    state_in = jnp.where(second, first_a * got + first_s, before_m)
    adjoint = jnp.where(second, before_m, last_u + last_a * got)
    return (state_in.reshape(forward.shape), adjoint.reshape(backward.shape))


def scattered_sum(partial, rows_axis, axis, width):
    chains, devices = (lax.axis_size(rows_axis), lax.axis_size(axis))
    chain, position = (lax.axis_index(rows_axis), lax.axis_index(axis))
    ring = RING if devices % RING == 0 else 1

    def label(t, turn):
        return t - t % ring + (t + turn) % ring

    def place(lab, turn):
        return lab - lab % ring + (lab - turn) % ring

    turn = chain % 2
    mine_label = label(position, turn)
    order = [place(lab, 1) for lab in range(devices)]
    rows = partial.shape[0]
    blocks = partial.reshape(rows, devices, width)
    blocks = jnp.where(turn == 1, blocks[:, order], blocks)
    bit = 1
    while bit < devices:
        count = blocks.shape[1]
        paired = blocks.reshape(rows, count // 2, 2, width)
        mine = mine_label & bit != 0
        keep = jnp.where(mine, paired[:, :, 1], paired[:, :, 0])
        send = jnp.where(mine, paired[:, :, 0], paired[:, :, 1])
        pairs = []
        for c in range(chains):
            for t in range(devices):
                partner = place(label(t, c % 2) ^ bit, c % 2)
                pairs.append((c * devices + t, c * devices + partner))
        blocks = keep + lax.ppermute(send, (rows_axis, axis), pairs)
        bit *= 2
    return blocks.reshape(rows, width)


def ssd_core(values, b_rows, c_rows, step_size, decay_rate, state):
    length, heads, head_dim = values.shape
    groups = b_rows.shape[1]
    per_group = heads // groups
    blocks = length // SPAN
    lower_mask = (jnp.arange(SPAN)[:, None] >= jnp.arange(SPAN)[None, :])[None]

    def blocked(array):
        return array.reshape((blocks, SPAN) + array.shape[1:])

    def ssd_advance(carry, item):
        value_blk, b_blk, c_blk, step_blk = item
        cums = jnp.cumsum(-step_blk * decay_rate[None, :], axis=0)
        diff = cums.T[:, :, None] - cums.T[:, None, :]
        weight = jnp.where(lower_mask, jnp.exp(jnp.where(lower_mask, diff, 0.0)), 0.0)
        scores = jnp.einsum("tgn,sgn->gts", c_blk, b_blk, precision=HIGH)
        scores = jnp.repeat(scores, per_group, axis=0)
        inputs = step_blk[:, :, None] * value_blk
        inside = jnp.einsum("hts,shp->thp", scores * weight, inputs, precision=HIGH)
        c_head = jnp.repeat(c_blk, per_group, axis=1)
        b_head = jnp.repeat(b_blk, per_group, axis=1)
        carried = jnp.exp(cums)[:, :, None] * jnp.einsum(
            "thn,hpn->thp", c_head, carry, precision=HIGH
        )
        tail = jnp.exp(cums[-1][None, :] - cums)
        fresh = jnp.einsum("shp,shn->hpn", tail[:, :, None] * inputs, b_head, precision=HIGH)
        carry = jnp.exp(cums[-1])[:, None, None] * carry + fresh
        return (carry, inside + carried)

    final, outputs = lax.scan(
        jax.checkpoint(ssd_advance),
        state,
        (blocked(values), blocked(b_rows), blocked(c_rows), blocked(step_size)),
    )
    return (outputs.reshape(length, heads, head_dim), final)


def local_states(values, b_rows, step_size, decay_rate):
    length, heads, head_dim = values.shape
    groups = b_rows.shape[1]
    per_group = heads // groups
    blocks = length // SPAN

    def blocked(array):
        return array.reshape((blocks, SPAN) + array.shape[1:])

    def local_advance(carry, item):
        value_blk, b_blk, step_blk = item
        cums = jnp.cumsum(-step_blk * decay_rate[None, :], axis=0)
        tail = jnp.exp(cums[-1][None, :] - cums)
        b_head = jnp.repeat(b_blk, per_group, axis=1)
        inputs = (tail * step_blk)[:, :, None] * value_blk
        fresh = jnp.einsum("shp,shn->hpn", inputs, b_head, precision=HIGH)
        return (jnp.exp(cums[-1])[:, None, None] * carry + fresh, None)

    start = jnp.zeros((heads, head_dim, STATE), jnp.float32)
    final, unused = lax.scan(
        local_advance, start, (blocked(values), blocked(b_rows), blocked(step_size))
    )
    return final


def local_adjoint(d_mixed, c_rows, step_size, decay_rate):
    length, heads, head_dim = d_mixed.shape
    groups = c_rows.shape[1]
    per_group = heads // groups
    blocks = length // SPAN

    def blocked(array):
        return array.reshape((blocks, SPAN) + array.shape[1:])

    def retreat(carry, item):
        grad_blk, c_blk, step_blk = item
        cums = jnp.cumsum(-step_blk * decay_rate[None, :], axis=0)
        c_head = jnp.repeat(c_blk, per_group, axis=1)
        weighted = jnp.exp(cums)[:, :, None] * grad_blk
        term = jnp.einsum("thp,thn->hpn", weighted, c_head, precision=HIGH)
        return (term + jnp.exp(cums[-1])[:, None, None] * carry, None)

    start = jnp.zeros((heads, head_dim, STATE), jnp.float32)
    final, unused = lax.scan(
        retreat, start, (blocked(d_mixed), blocked(c_rows), blocked(step_size)), reverse=True
    )
    return final


def doubled_rows(x, axis, order):
    devices, position = (lax.axis_size(axis), lax.axis_index(axis))
    for b in order:
        bit = 1 << b
        other = lax.ppermute(x, axis, [(i, i ^ bit) for i in range(devices)])
        low = position & bit == 0
        x = jnp.where(low, jnp.concatenate([x, other], 0), jnp.concatenate([other, x], 0))
    rows = x.shape[0] // devices
    x = x.reshape((2,) * len(order) + (rows,) + x.shape[1:])
    axes = [len(order) - 1 - order.index(b) for b in reversed(range(len(order)))]
    x = jnp.transpose(x, axes + list(range(len(order), x.ndim)))
    return x.reshape((devices * rows,) + x.shape[len(order) + 1 :])


def row_block(w, index, size):
    return lax.dynamic_slice_in_dim(w, index * size, size, axis=0)


def per_device(tokens, w_in, w_bc, w_dt, dt_bias, decay_rate, skip_gain, w_out, cotangent):
    devices = lax.axis_size("tp")
    rows, width = tokens.shape
    heads = decay_rate.shape[0]
    inner = w_in.shape[1]
    pair_cols = w_bc.shape[1]
    groups = pair_cols // (2 * STATE)
    out_cols = w_out.shape[0]
    w_all = lax.all_gather(
        jnp.concatenate([w_out.T, w_in, w_bc, w_dt], axis=1), "ctx", axis=0, tiled=True
    )
    bits = devices.bit_length() - 1
    pieces = doubled_rows(
        jnp.concatenate([tokens, cotangent], axis=1), "tp", list(reversed(range(bits)))
    )
    projected = None
    d_flat = None
    for k in range(devices):
        block = w_all[k * width : (k + 1) * width]
        piece = pieces[k * rows : (k + 1) * rows]
        term = jnp.dot(piece[:, :width], block[:, out_cols:], preferred_element_type=jnp.float32)
        projected = term if projected is None else projected + term
        term = jnp.dot(piece[:, width:], block[:, :out_cols], preferred_element_type=jnp.float32)
        d_flat = term if d_flat is None else d_flat + term
    values = projected[:, :inner].astype(jnp.bfloat16)
    pairs = projected[:, inner : inner + pair_cols].astype(jnp.bfloat16)
    pre_step = projected[:, inner + pair_cols :] + dt_bias[None, :]
    step_size = jax.nn.softplus(pre_step)
    value_f = values.astype(jnp.float32).reshape(rows, heads, HEADDIM)
    paired = pairs.astype(jnp.float32).reshape(rows, groups, 2, STATE)
    b_rows = paired[:, :, 0]
    c_rows = paired[:, :, 1]
    end_state = local_states(value_f, b_rows, step_size, decay_rate)
    decay_total = jnp.exp(-jnp.sum(step_size * decay_rate[None, :], axis=0))
    d_mixed = d_flat.reshape(rows, heads, HEADDIM)
    own_adjoint = local_adjoint(d_mixed, c_rows, step_size, decay_rate)
    state_in, adjoint = both_carries(decay_total, end_state, own_adjoint, "ctx")

    def with_state(vals, brows, crows, steps):
        return ssd_core(vals, brows, crows, steps, decay_rate, state_in)

    (core_out, core_end), pullback = jax.vjp(with_state, value_f, b_rows, c_rows, step_size)
    mixed = (
        (core_out + skip_gain[None, :, None] * value_f).reshape(rows, inner).astype(jnp.bfloat16)
    )
    partial_out = lax.dot_general(
        mixed, w_all[:, :out_cols], (((1,), (1,)), ((), ())), preferred_element_type=jnp.float32
    )
    output = scattered_sum(partial_out, "ctx", "tp", width).astype(jnp.bfloat16)
    grads = pullback((d_mixed, adjoint))
    d_values = grads[0] + skip_gain[None, :, None] * d_mixed
    d_pre = grads[3] * jax.nn.sigmoid(pre_step)
    d_pairs = jnp.stack([grads[1], grads[2]], axis=2).reshape(rows, pair_cols)
    d_cat = jnp.concatenate(
        [
            d_values.reshape(rows, inner).astype(jnp.bfloat16),
            d_pairs.astype(jnp.bfloat16),
            d_pre.astype(jnp.bfloat16),
        ],
        axis=1,
    )
    partial_grad = lax.dot_general(
        d_cat, w_all[:, out_cols:], (((1,), (1,)), ((), ())), preferred_element_type=jnp.float32
    )
    grad = scattered_sum(partial_grad, "ctx", "tp", width).astype(jnp.bfloat16)
    return (output, grad)


def solution(mesh):
    placed = (
        P("ctx", "tp"),
        P("ctx", "tp"),
        P("ctx", "tp"),
        P("ctx", "tp"),
        P("tp"),
        P("tp"),
        P("tp"),
        P("tp", "ctx"),
        P("ctx", "tp"),
    )
    return jax.shard_map(
        per_device,
        mesh=mesh,
        in_specs=placed,
        out_specs=(P("ctx", "tp"), P("ctx", "tp")),
        check_vma=False,
    )
```

profile of v0, /device:TPU:9, one launch (start us, length us, event | category | flops | bytes accessed | tf_op | source)
XLA Modules:
  0.0 366.3 jit_solution(14436932147277387907)
XLA Ops:
  11.3 6.6 %collective-permute-start = (bf16[256,512]{1,0:T(8,128)(2,1)S(1)}, bf16[256,512]{1,0:T(8,128)(2,1)S(1)}, u32[]{:S(2)}, u32[]{:S(2)}) collective-permute-start(bf16[256,512]{1,0:T(8,128)(2,1)S(1)} %constant_dynamic-update-slice_fusion), channel_id=1, source_target_pairs={{0,4},{1,5},{2,6},{3,7},{4,0},{5,1},{6,2},{7,3},{8,12},{9,13},{10,... | collective-permute-start | bytes 786440 | tf_op jit(solution)/shard_map/ppermute | solution.py:184
  17.8 9.1 %collective-permute-done = bf16[256,512]{1,0:T(8,128)(2,1)S(1)} collective-permute-done((bf16[256,512]{1,0:T(8,128)(2,1)S(1)}, bf16[256,512]{1,0:T(8,128)(2,1)S(1)}, u32[]{:S(2)}, u32[]{:S(2)}) %collective-permute-start) | collective-permute-done | bytes 262176 | tf_op jit(solution)/shard_map/ppermute | solution.py:184
  27.1 4.7 %collective-permute-start.1 = (bf16[512,512]{1,0:T(8,128)(2,1)S(1)}, bf16[512,512]{1,0:T(8,128)(2,1)S(1)}, u32[]{:S(2)}, u32[]{:S(2)}) collective-permute-start(bf16[512,512]{1,0:T(8,128)(2,1)S(1)} %maximum_select_fusion.2), channel_id=1, source_target_pairs={{0,2},{1,3},{2,0},{3,1},{4,6},{5,7},{6,4},{7,5},{8,10},{9,11},{10,... | collective-permute-start | bytes 1572872 | tf_op jit(solution)/shard_map/ppermute | solution.py:184
  31.8 8.0 %collective-permute-done.1 = bf16[512,512]{1,0:T(8,128)(2,1)S(1)} collective-permute-done((bf16[512,512]{1,0:T(8,128)(2,1)S(1)}, bf16[512,512]{1,0:T(8,128)(2,1)S(1)}, u32[]{:S(2)}, u32[]{:S(2)}) %collective-permute-start.1) | collective-permute-done | bytes 524320 | tf_op jit(solution)/shard_map/ppermute | solution.py:184
  43.4 18.3 %collective-permute-done.2 = bf16[1024,512]{1,0:T(8,128)(2,1)S(1)} collective-permute-done((bf16[1024,512]{1,0:T(8,128)(2,1)S(1)}, bf16[1024,512]{1,0:T(8,128)(2,1)S(1)}, u32[]{:S(2)}, u32[]{:S(2)}) %collective-permute-start.2) | collective-permute-done | bytes 1048608 | tf_op jit(solution)/shard_map/ppermute | solution.py:184
  62.5 75.4 %all-gather.2.cloned.1.call-done = bf16[2048,1288]{1,0:T(8,128)(2,1)} async-done(((bf16[32,1288]{1,0:T(8,128)(2,1)}), bf16[2048,1288]{1,0:T(8,128)(2,1)}) %all-gather.2.cloned.1.call-update) | async-done | bytes 5275664 | tf_op jit(solution)/shard_map/all_gather | solution.py:206
  168.6 4.3 %collective-permute-start.4 = (f32[8,8320]{1,0:T(8,128)}, f32[8,8320]{1,0:T(8,128)S(1)}, u32[]{:S(2)}, u32[]{:S(2)}) collective-permute-start(f32[8,8320]{1,0:T(8,128)} %pad_maximum_fusion.1), channel_id=1, source_target_pairs={{0,16},{8,24},{16,0},{24,8},{32,48},{40,56},{48,32},{56,40},{64,80... | collective-permute-start | bytes 798728 | tf_op jit(solution)/shard_map/ppermute | solution.py:45
  172.9 6.7 %collective-permute-done.4 = f32[8,8320]{1,0:T(8,128)S(1)} collective-permute-done((f32[8,8320]{1,0:T(8,128)}, f32[8,8320]{1,0:T(8,128)S(1)}, u32[]{:S(2)}, u32[]{:S(2)}) %collective-permute-start.4) | collective-permute-done | bytes 266272 | tf_op jit(solution)/shard_map/ppermute | solution.py:45
  180.7 4.3 %collective-permute-start.5 = (f32[8,8320]{1,0:T(8,128)}, f32[8,8320]{1,0:T(8,128)}, u32[]{:S(2)}, u32[]{:S(2)}) collective-permute-start(f32[8,8320]{1,0:T(8,128)} %pad_maximum_fusion.2), channel_id=1, source_target_pairs={{0,32},{8,40},{16,48},{24,56},{32,0},{40,8},{48,16},{56,24},{64,96... | collective-permute-start | bytes 798728 | tf_op jit(solution)/shard_map/ppermute | solution.py:45
  184.9 12.0 %collective-permute-done.5 = f32[8,8320]{1,0:T(8,128)} collective-permute-done((f32[8,8320]{1,0:T(8,128)}, f32[8,8320]{1,0:T(8,128)}, u32[]{:S(2)}, u32[]{:S(2)}) %collective-permute-start.5) | collective-permute-done | bytes 266272 | tf_op jit(solution)/shard_map/ppermute | solution.py:45
  199.5 6.3 %collective-permute-start.6 = (f32[8,8320]{1,0:T(8,128)}, f32[8,8320]{1,0:T(8,128)}, u32[]{:S(2)}, u32[]{:S(2)}) collective-permute-start(f32[8,8320]{1,0:T(8,128)} %pad_maximum_fusion.3), channel_id=1, source_target_pairs={{0,64},{8,72},{16,80},{24,88},{32,96},{40,104},{48,112},{56,120},{... | collective-permute-start | bytes 798728 | tf_op jit(solution)/shard_map/ppermute | solution.py:45
  206.5 11.8 %collective-permute-done.6 = f32[8,8320]{1,0:T(8,128)} collective-permute-done((f32[8,8320]{1,0:T(8,128)}, f32[8,8320]{1,0:T(8,128)}, u32[]{:S(2)}, u32[]{:S(2)}) %collective-permute-start.6) | collective-permute-done | bytes 266272 | tf_op jit(solution)/shard_map/ppermute | solution.py:45
  224.4 4.7 %collective-permute-done.7 = f32[8,8320]{1,0:T(8,128)} collective-permute-done((f32[8,8320]{1,0:T(8,128)}, f32[8,8320]{1,0:T(8,128)}, u32[]{:S(2)}, u32[]{:S(2)}) %collective-permute-start.7) | collective-permute-done | bytes 266272 | tf_op jit(solution)/shard_map/ppermute | solution.py:45
  232.3 6.8 %collective-permute-done.8 = f32[8,8192]{1,0:T(8,128)S(1)} collective-permute-done((f32[8,8192]{1,0:T(8,128)S(1)}, f32[8,8192]{1,0:T(8,128)S(1)}, u32[]{:S(2)}, u32[]{:S(2)}) %collective-permute-start.8) | collective-permute-done | bytes 262176 | tf_op jit(solution)/shard_map/ppermute | solution.py:40
  240.4 6.8 %collective-permute-start.9 = (f32[8,8192]{1,0:T(8,128)S(1)}, f32[8,8192]{1,0:T(8,128)S(1)}, u32[]{:S(2)}, u32[]{:S(2)}) collective-permute-start(f32[8,8192]{1,0:T(8,128)S(1)} %add_select_fusion), channel_id=1, source_target_pairs={{0,8},{8,0},{16,24},{24,16},{32,40},{40,32},{48,56},{56,48},{64,72... | collective-permute-start | bytes 786440 | tf_op jit(solution)/shard_map/ppermute | solution.py:54
  265.4 3.3 fusion
  274.6 3.7 %gather_fusion.1 = f32[8,256,256]{2,1,0:T(8,128)} fusion(f32[256,8,256]{2,0,1:T(8,128)} %bitcast.319, s32[1024]{0:T(1024)} %pad_clamp_fusion), kind=kCustom, calls=%fused_computation.1 | custom fusion | bytes 4194336 | tf_op jit(solution)/shard_map/gather | solution.py:76
  283.7 3.7 collective-permute-start.10
  289.2 3.2 collective-permute-start.13
  292.4 8.5 %collective-permute-done.10 = f32[256,4,256]{2,0,1:T(8,128)} collective-permute-done((f32[256,4,256]{2,0,1:T(8,128)}, f32[256,4,256]{2,0,1:T(8,128)}, u32[]{:S(2)}, u32[]{:S(2)}) %collective-permute-start.10) | collective-permute-done | bytes 1048608 | tf_op jit(solution)/shard_map/ppermute | solution.py:89
  305.4 9.8 %collective-permute-done.13 = f32[256,4,256]{2,0,1:T(8,128)} collective-permute-done((f32[256,4,256]{2,0,1:T(8,128)}, f32[256,4,256]{2,0,1:T(8,128)}, u32[]{:S(2)}, u32[]{:S(2)}) %collective-permute-start.13) | collective-permute-done | bytes 1048608 | tf_op jit(solution)/shard_map/ppermute | solution.py:89
  320.9 12.9 %collective-permute-start.12 = (f32[256,1,256]{2,0,1:T(8,128)S(1)}, f32[256,1,256]{2,0,1:T(8,128)S(1)}, u32[]{:S(2)}, u32[]{:S(2)}) collective-permute-start(f32[256,1,256]{2,0,1:T(8,128)S(1)} %select_bitcast_fusion.6), channel_id=1, source_target_pairs={{0,4},{1,5},{2,6},{3,7},{4,0},{5,1},{6,2},{7,3},{8,12},{9,13},{10,... | collective-permute-start | bytes 786440 | tf_op jit(solution)/shard_map/ppermute | solution.py:89
  336.9 7.8 %collective-permute-start.15 = (f32[256,1,256]{2,0,1:T(8,128)S(1)}, f32[256,1,256]{2,0,1:T(8,128)S(1)}, u32[]{:S(2)}, u32[]{:S(2)}) collective-permute-start(f32[256,1,256]{2,0,1:T(8,128)S(1)} %select_bitcast_fusion.4), channel_id=1, source_target_pairs={{0,4},{1,5},{2,6},{3,7},{4,0},{5,1},{6,2},{7,3},{8,12},{9,13},{10,... | collective-permute-start | bytes 786440 | tf_op jit(solution)/shard_map/ppermute | solution.py:89
  345.4 13.3 %collective-permute-done.15 = f32[256,1,256]{2,0,1:T(8,128)S(1)} collective-permute-done((f32[256,1,256]{2,0,1:T(8,128)S(1)}, f32[256,1,256]{2,0,1:T(8,128)S(1)}, u32[]{:S(2)}, u32[]{:S(2)}) %collective-permute-start.15) | collective-permute-done | bytes 262176 | tf_op jit(solution)/shard_map/ppermute | solution.py:89
  (218 shorter events, 99.3 us)
Async XLA Ops:
  7.2 130.8 %all-gather.2.cloned.1.call-start = ((), (), s32[]{:S(2)}) async-start(), calls=%async_computation | async-start | bytes 5857280 | tf_op jit(solution)/shard_map/all_gather | solution.py:206
  11.3 15.6 %collective-permute-start = (bf16[256,512]{1,0:T(8,128)(2,1)S(1)}, bf16[256,512]{1,0:T(8,128)(2,1)S(1)}, u32[]{:S(2)}, u32[]{:S(2)}) collective-permute-start(bf16[256,512]{1,0:T(8,128)(2,1)S(1)} %constant_dynamic-update-slice_fusion), channel_id=1, source_target_pairs={{0,4},{1,5},{2,6},{3,7},{4,0},{5,1},{6,2},{7,3},{8,12},{9,13},{10,... | collective-permute-start | bytes 786440 | tf_op jit(solution)/shard_map/ppermute | solution.py:184
  27.1 12.7 %collective-permute-start.1 = (bf16[512,512]{1,0:T(8,128)(2,1)S(1)}, bf16[512,512]{1,0:T(8,128)(2,1)S(1)}, u32[]{:S(2)}, u32[]{:S(2)}) collective-permute-start(bf16[512,512]{1,0:T(8,128)(2,1)S(1)} %maximum_select_fusion.2), channel_id=1, source_target_pairs={{0,2},{1,3},{2,0},{3,1},{4,6},{5,7},{6,4},{7,5},{8,10},{9,11},{10,... | collective-permute-start | bytes 1572872 | tf_op jit(solution)/shard_map/ppermute | solution.py:184
  40.3 21.5 %collective-permute-start.2 = (bf16[1024,512]{1,0:T(8,128)(2,1)S(1)}, bf16[1024,512]{1,0:T(8,128)(2,1)S(1)}, u32[]{:S(2)}, u32[]{:S(2)}) collective-permute-start(bf16[1024,512]{1,0:T(8,128)(2,1)S(1)} %maximum_select_fusion.1), channel_id=1, source_target_pairs={{0,1},{1,0},{2,3},{3,2},{4,5},{5,4},{6,7},{7,6},{8,9},{9,8},{10,11... | collective-permute-start | bytes 3145736 | tf_op jit(solution)/shard_map/ppermute | solution.py:184
  62.5 81.6 %copy-start.6 = (bf16[2,2,2,256,512]{4,3,2,1,0:T(8,128)(2,1)}, bf16[2,2,2,256,512]{4,3,2,1,0:T(8,128)(2,1)S(1)}, u32[]{:S(2)}) copy-start(bf16[2,2,2,256,512]{4,3,2,1,0:T(8,128)(2,1)S(1)} %copy.125) | copy-start | bytes 6291460
  163.3 4.0 %collective-permute-start.3 = (f32[8,16512]{1,0:T(8,128)}, f32[8,16512]{1,0:T(8,128)S(1)}, u32[]{:S(2)}, u32[]{:S(2)}) collective-permute-start(f32[8,16512]{1,0:T(8,128)} %pad_maximum_fusion), channel_id=1, source_target_pairs={{0,8},{8,0},{16,24},{24,16},{32,40},{40,32},{48,56},{56,48},{64,72... | collective-permute-start | bytes 1585160 | tf_op jit(solution)/shard_map/ppermute | solution.py:21
  168.6 54.3 %copy-start.30 = (s32[8]{0:T(128)S(1)}, s32[8]{0:T(128)}, u32[]{:S(2)}) copy-start(s32[8]{0:T(128)} %constant.154) | copy-start | bytes 100
  168.6 11.1 %collective-permute-start.4 = (f32[8,8320]{1,0:T(8,128)}, f32[8,8320]{1,0:T(8,128)S(1)}, u32[]{:S(2)}, u32[]{:S(2)}) collective-permute-start(f32[8,8320]{1,0:T(8,128)} %pad_maximum_fusion.1), channel_id=1, source_target_pairs={{0,16},{8,24},{16,0},{24,8},{32,48},{40,56},{48,32},{56,40},{64,80... | collective-permute-start | bytes 798728 | tf_op jit(solution)/shard_map/ppermute | solution.py:45
  179.8 43.7 %copy-start.29 = (f32[8]{0:T(128)S(1)}, f32[8]{0:T(128)}, u32[]{:S(2)}) copy-start(f32[8]{0:T(128)} %param.17) | copy-start | bytes 100
  179.8 44.5 %copy-start.12 = (bf16[256,256]{0,1:T(8,128)(2,1)S(1)}, bf16[256,256]{0,1:T(8,128)(2,1)}, u32[]{:S(2)}) copy-start(bf16[256,256]{0,1:T(8,128)(2,1)} %copy-done.11) | copy-start | bytes 393220
  180.7 16.2 %collective-permute-start.5 = (f32[8,8320]{1,0:T(8,128)}, f32[8,8320]{1,0:T(8,128)}, u32[]{:S(2)}, u32[]{:S(2)}) collective-permute-start(f32[8,8320]{1,0:T(8,128)} %pad_maximum_fusion.2), channel_id=1, source_target_pairs={{0,32},{8,40},{16,48},{24,56},{32,0},{40,8},{48,16},{56,24},{64,96... | collective-permute-start | bytes 798728 | tf_op jit(solution)/shard_map/ppermute | solution.py:45
  199.5 18.8 %collective-permute-start.6 = (f32[8,8320]{1,0:T(8,128)}, f32[8,8320]{1,0:T(8,128)}, u32[]{:S(2)}, u32[]{:S(2)}) collective-permute-start(f32[8,8320]{1,0:T(8,128)} %pad_maximum_fusion.3), channel_id=1, source_target_pairs={{0,64},{8,72},{16,80},{24,88},{32,96},{40,104},{48,112},{56,120},{... | collective-permute-start | bytes 798728 | tf_op jit(solution)/shard_map/ppermute | solution.py:45
  219.1 28.1 %copy-start.17 = (f32[8,2,128]{2,0,1:T(8,128)S(1)}, f32[8,2,128]{2,0,1:T(8,128)}, u32[]{:S(2)}) copy-start(f32[8,2,128]{2,0,1:T(8,128)} %copy-done.16) | copy-start | bytes 24580
  219.1 28.2 %copy-start.22 = (f32[8,2]{0,1:T(2,128)S(1)}, f32[8,2]{0,1:T(2,128)}, u32[]{:S(2)}) copy-start(f32[8,2]{0,1:T(2,128)} %copy-done.21) | copy-start | bytes 196
  220.9 8.2 %collective-permute-start.7 = (f32[8,8320]{1,0:T(8,128)}, f32[8,8320]{1,0:T(8,128)}, u32[]{:S(2)}, u32[]{:S(2)}) collective-permute-start(f32[8,8320]{1,0:T(8,128)} %pad_maximum_fusion.4), channel_id=1, source_target_pairs={{0,128},{8,136},{16,144},{24,152},{32,160},{40,168},{48,176},{56,1... | collective-permute-start | bytes 798728 | tf_op jit(solution)/shard_map/ppermute | solution.py:45
  230.9 8.1 %collective-permute-start.8 = (f32[8,8192]{1,0:T(8,128)S(1)}, f32[8,8192]{1,0:T(8,128)S(1)}, u32[]{:S(2)}, u32[]{:S(2)}) collective-permute-start(f32[8,8192]{1,0:T(8,128)S(1)} %add_select_fusion.4), channel_id=1, source_target_pairs={{0,256},{16,272},{32,288},{48,304},{64,320},{80,336},{96,352},{112... | collective-permute-start | bytes 786440 | tf_op jit(solution)/shard_map/ppermute | solution.py:40
  240.4 9.2 %collective-permute-start.9 = (f32[8,8192]{1,0:T(8,128)S(1)}, f32[8,8192]{1,0:T(8,128)S(1)}, u32[]{:S(2)}, u32[]{:S(2)}) collective-permute-start(f32[8,8192]{1,0:T(8,128)S(1)} %add_select_fusion), channel_id=1, source_target_pairs={{0,8},{8,0},{16,24},{24,16},{32,40},{40,32},{48,56},{56,48},{64,72... | collective-permute-start | bytes 786440 | tf_op jit(solution)/shard_map/ppermute | solution.py:54
  283.7 17.2 %collective-permute-start.10 = (f32[256,4,256]{2,0,1:T(8,128)}, f32[256,4,256]{2,0,1:T(8,128)}, u32[]{:S(2)}, u32[]{:S(2)}) collective-permute-start(f32[256,4,256]{2,0,1:T(8,128)} %select_bitcast_fusion.1), channel_id=1, source_target_pairs={{0,1},{1,0},{2,3},{3,2},{4,5},{5,4},{6,7},{7,6},{8,11},{9,10},{10,... | collective-permute-start | bytes 3145736 | tf_op jit(solution)/shard_map/ppermute | solution.py:89
  289.2 26.0 %collective-permute-start.13 = (f32[256,4,256]{2,0,1:T(8,128)}, f32[256,4,256]{2,0,1:T(8,128)}, u32[]{:S(2)}, u32[]{:S(2)}) collective-permute-start(f32[256,4,256]{2,0,1:T(8,128)} %select_bitcast_fusion), channel_id=1, source_target_pairs={{0,1},{1,0},{2,3},{3,2},{4,5},{5,4},{6,7},{7,6},{8,11},{9,10},{10,... | collective-permute-start | bytes 3145736 | tf_op jit(solution)/shard_map/ppermute | solution.py:89
  303.1 17.7 %collective-permute-start.11 = (f32[256,2,256]{2,0,1:T(8,128)S(1)}, f32[256,2,256]{2,0,1:T(8,128)S(1)}, u32[]{:S(2)}, u32[]{:S(2)}) collective-permute-start(f32[256,2,256]{2,0,1:T(8,128)S(1)} %select_bitcast_fusion.3), channel_id=1, source_target_pairs={{0,2},{1,3},{2,0},{3,1},{4,6},{5,7},{6,4},{7,5},{8,10},{9,11},{10,... | collective-permute-start | bytes 1572872 | tf_op jit(solution)/shard_map/ppermute | solution.py:89
  318.6 17.2 %copy-start.3 = (f32[256,4,256]{2,0,1:T(8,128)S(1)}, f32[256,4,256]{2,0,1:T(8,128)}, u32[]{:S(2)}) copy-start(f32[256,4,256]{2,0,1:T(8,128)} %copy-done.2) | copy-start | bytes 3145732
  318.6 17.1 %collective-permute-start.14 = (f32[256,2,256]{2,0,1:T(8,128)}, f32[256,2,256]{2,0,1:T(8,128)}, u32[]{:S(2)}, u32[]{:S(2)}) collective-permute-start(f32[256,2,256]{2,0,1:T(8,128)} %select_bitcast_fusion.2), channel_id=1, source_target_pairs={{0,2},{1,3},{2,0},{3,1},{4,6},{5,7},{6,4},{7,5},{8,10},{9,11},{10,... | collective-permute-start | bytes 1572872 | tf_op jit(solution)/shard_map/ppermute | solution.py:89
  320.9 23.8 %collective-permute-start.12 = (f32[256,1,256]{2,0,1:T(8,128)S(1)}, f32[256,1,256]{2,0,1:T(8,128)S(1)}, u32[]{:S(2)}, u32[]{:S(2)}) collective-permute-start(f32[256,1,256]{2,0,1:T(8,128)S(1)} %select_bitcast_fusion.6), channel_id=1, source_target_pairs={{0,4},{1,5},{2,6},{3,7},{4,0},{5,1},{6,2},{7,3},{8,12},{9,13},{10,... | collective-permute-start | bytes 786440 | tf_op jit(solution)/shard_map/ppermute | solution.py:89
  336.9 21.8 %collective-permute-start.15 = (f32[256,1,256]{2,0,1:T(8,128)S(1)}, f32[256,1,256]{2,0,1:T(8,128)S(1)}, u32[]{:S(2)}, u32[]{:S(2)}) collective-permute-start(f32[256,1,256]{2,0,1:T(8,128)S(1)} %select_bitcast_fusion.4), channel_id=1, source_target_pairs={{0,4},{1,5},{2,6},{3,7},{4,0},{5,1},{6,2},{7,3},{8,12},{9,13},{10,... | collective-permute-start | bytes 786440 | tf_op jit(solution)/shard_map/ppermute | solution.py:89
  (27 other events, 125.3 us)
Sparse Core Ops, SparseCore 0:
  10.7 127.1 all-gather.1
where the time goes:
time: 368 us; the launch traced here: 366 us
  waiting for transfers between devices  188 us (51%)
  starting transfers between devices  73.5 us (20%)
  matrix products  35.3 us (10%)
  other arithmetic  32.3 us (9%)
  local copies, waits for them, and re-layouts  22.1 us (6%)
  between operations  15 us (4%)
    all_gather x1, waiting for transfers between devices, per_device(): lax.all_gather(jnp.concatenate([w_out.T, w_in, w_bc, w_dt], axis=1), 'ctx...  75.4 us
    ppermute x3, waiting for transfers between devices, doubled_rows(): other = lax.ppermute(x, axis, [(i, i ^ bit) for i in range(devices)])  35.4 us
    ppermute x4, waiting for transfers between devices, both_carries(): got = lax.ppermute(message, axis, [(i, i ^ bit) for i in range(devices)])  35.2 us
    ppermute x6, waiting for transfers between devices, scattered_sum(): blocks = keep + lax.ppermute(send, (rows_axis, axis), pairs)  33.5 us
    ppermute x6, starting transfers between devices, scattered_sum(): blocks = keep + lax.ppermute(send, (rows_axis, axis), pairs)  32 us
    ppermute x4, starting transfers between devices, both_carries(): got = lax.ppermute(message, axis, [(i, i ^ bit) for i in range(devices)])  16.8 us
    ppermute x3, starting transfers between devices, doubled_rows(): other = lax.ppermute(x, axis, [(i, i ^ bit) for i in range(devices)])  14.3 us
    dot_general x8, matrix products, per_device(): jnp.dot(piece[:, width:], block[:, :out_cols], preferred_element_type=jnp...  10.3 us
  transfers between devices with their start and end apart: 17, of which 14 were waited for; matrix products, arithmetic and copies ran while one was open for 4% of the time, Pallas kernels for 0%

commit v1 on v0

--- a/solution.py
+++ b/solution.py
@@ -203,8 +203,16 @@
     pair_cols = w_bc.shape[1]
     groups = pair_cols // (2 * STATE)
     out_cols = w_out.shape[0]
-    w_all = lax.all_gather(
-        jnp.concatenate([w_out.T, w_in, w_bc, w_dt], axis=1), "ctx", axis=0, tiled=True
+    w_all = jnp.concatenate(
+        lax.all_to_all(
+            jnp.stack(
+                [jnp.concatenate([w_out.T, w_in, w_bc, w_dt], axis=1)] * lax.axis_size("ctx")
+            ),
+            "ctx",
+            0,
+            0,
+        ),
+        axis=0,
     )
     bits = devices.bit_length() - 1
     pieces = doubled_rows(

time: 368 us -> 438 us (1.19)
  the two profiles are of different devices: /device:TPU:9 before, /device:TPU:56 now
where the time goes in v1:
time: 438 us; the launch traced here: 437 us
  waiting for transfers between devices  243 us (55%)
  starting transfers between devices  87.4 us (20%)
  other arithmetic  36.8 us (8%)
  matrix products  34.5 us (8%)
  local copies, waits for them, and re-layouts  33.7 us (8%)
    ppermute x3, waiting for transfers between devices, doubled_rows(): other = lax.ppermute(x, axis, [(i, i ^ bit) for i in range(devices)])  161 us
    ppermute x4, waiting for transfers between devices, both_carries(): got = lax.ppermute(message, axis, [(i, i ^ bit) for i in range(devices)])  35 us
    ppermute x6, waiting for transfers between devices, scattered_sum(): blocks = keep + lax.ppermute(send, (rows_axis, axis), pairs)  34.8 us
    ppermute x4, starting transfers between devices, both_carries(): got = lax.ppermute(message, axis, [(i, i ^ bit) for i in range(devices)])  27.2 us
    ppermute x6, starting transfers between devices, scattered_sum(): blocks = keep + lax.ppermute(send, (rows_axis, axis), pairs)  27.2 us
    all_to_all x1, starting transfers between devices, per_device(): lax.all_to_all(jnp.stack([jnp.concatenate([w_out.T, w_in, w_bc, w_dt], ax...  14.6 us
    ppermute x3, starting transfers between devices, doubled_rows(): other = lax.ppermute(x, axis, [(i, i ^ bit) for i in range(devices)])  13 us
    ppermute x1, waiting for transfers between devices, both_carries(): got_m = lax.ppermute(total_m, axis, wanted)  10.2 us
  transfers between devices with their start and end apart: 17, of which 13 were waited for; matrix products, arithmetic and copies ran while one was open for 6% of the time, Pallas kernels for 0%

profile of v1, /device:TPU:56, one launch (start us, length us, event | category | flops | bytes accessed | tf_op | source)
XLA Modules:
  0.0 436.8 jit_solution(8335467657005837384)
XLA Ops:
  5.1 14.6 %all-to-all-start = ((bf16[64,32,1288]{2,1,0:T(8,128)(2,1)}), bf16[64,32,1288]{2,1,0:T(8,128)(2,1)}, u32[]{:S(2)}, u32[]{:S(2)}) async-start(bf16[64,32,1288]{2,1,0:T(8,128)(2,1)} %stack.5), calls=%async_computation | async-start | bytes 11534336 | tf_op jit(solution)/shard_map/all_to_all | solution.py:207
  19.8 4.7 %collective-permute-start = (bf16[256,512]{1,0:T(8,128)(2,1)S(1)}, bf16[256,512]{1,0:T(8,128)(2,1)S(1)}, u32[]{:S(2)}, u32[]{:S(2)}) collective-permute-start(bf16[256,512]{1,0:T(8,128)(2,1)S(1)} %constant_dynamic-update-slice_fusion), channel_id=1, source_target_pairs={{0,4},{1,5},{2,6},{3,7},{4,0},{5,1},{6,2},{7,3},{8,12},{9,13},{10,... | collective-permute-start | bytes 786440 | tf_op jit(solution)/shard_map/ppermute | solution.py:184
  24.6 126.5 %collective-permute-done = bf16[256,512]{1,0:T(8,128)(2,1)S(1)} collective-permute-done((bf16[256,512]{1,0:T(8,128)(2,1)S(1)}, bf16[256,512]{1,0:T(8,128)(2,1)S(1)}, u32[]{:S(2)}, u32[]{:S(2)}) %collective-permute-start) | collective-permute-done | bytes 262176 | tf_op jit(solution)/shard_map/ppermute | solution.py:184
  151.3 4.9 %collective-permute-start.1 = (bf16[512,512]{1,0:T(8,128)(2,1)S(1)}, bf16[512,512]{1,0:T(8,128)(2,1)S(1)}, u32[]{:S(2)}, u32[]{:S(2)}) collective-permute-start(bf16[512,512]{1,0:T(8,128)(2,1)S(1)} %maximum_select_fusion.2), channel_id=1, source_target_pairs={{0,2},{1,3},{2,0},{3,1},{4,6},{5,7},{6,4},{7,5},{8,10},{9,11},{10,... | collective-permute-start | bytes 1572872 | tf_op jit(solution)/shard_map/ppermute | solution.py:184
  156.3 11.9 %collective-permute-done.1 = bf16[512,512]{1,0:T(8,128)(2,1)S(1)} collective-permute-done((bf16[512,512]{1,0:T(8,128)(2,1)S(1)}, bf16[512,512]{1,0:T(8,128)(2,1)S(1)}, u32[]{:S(2)}, u32[]{:S(2)}) %collective-permute-start.1) | collective-permute-done | bytes 524320 | tf_op jit(solution)/shard_map/ppermute | solution.py:184
  172.0 22.2 %collective-permute-done.2 = bf16[1024,512]{1,0:T(8,128)(2,1)S(1)} collective-permute-done((bf16[1024,512]{1,0:T(8,128)(2,1)S(1)}, bf16[1024,512]{1,0:T(8,128)(2,1)S(1)}, u32[]{:S(2)}, u32[]{:S(2)}) %collective-permute-start.2) | collective-permute-done | bytes 1048608 | tf_op jit(solution)/shard_map/ppermute | solution.py:184
  228.8 5.5 %collective-permute-start.4 = (f32[8,8320]{1,0:T(8,128)}, f32[8,8320]{1,0:T(8,128)}, u32[]{:S(2)}, u32[]{:S(2)}) collective-permute-start(f32[8,8320]{1,0:T(8,128)} %pad_maximum_fusion.1), channel_id=1, source_target_pairs={{0,16},{8,24},{16,0},{24,8},{32,48},{40,56},{48,32},{56,40},{64,80... | collective-permute-start | bytes 798728 | tf_op jit(solution)/shard_map/ppermute | solution.py:45
  234.2 7.0 %collective-permute-done.4 = f32[8,8320]{1,0:T(8,128)} collective-permute-done((f32[8,8320]{1,0:T(8,128)}, f32[8,8320]{1,0:T(8,128)}, u32[]{:S(2)}, u32[]{:S(2)}) %collective-permute-start.4) | collective-permute-done | bytes 266272 | tf_op jit(solution)/shard_map/ppermute | solution.py:45
  243.9 8.2 %collective-permute-start.5 = (f32[8,8320]{1,0:T(8,128)}, f32[8,8320]{1,0:T(8,128)}, u32[]{:S(2)}, u32[]{:S(2)}) collective-permute-start(f32[8,8320]{1,0:T(8,128)} %pad_maximum_fusion.2), channel_id=1, source_target_pairs={{0,32},{8,40},{16,48},{24,56},{32,0},{40,8},{48,16},{56,24},{64,96... | collective-permute-start | bytes 798728 | tf_op jit(solution)/shard_map/ppermute | solution.py:45
  252.1 11.9 %collective-permute-done.5 = f32[8,8320]{1,0:T(8,128)} collective-permute-done((f32[8,8320]{1,0:T(8,128)}, f32[8,8320]{1,0:T(8,128)}, u32[]{:S(2)}, u32[]{:S(2)}) %collective-permute-start.5) | collective-permute-done | bytes 266272 | tf_op jit(solution)/shard_map/ppermute | solution.py:45
  266.6 11.7 %collective-permute-start.6 = (f32[8,8320]{1,0:T(8,128)}, f32[8,8320]{1,0:T(8,128)}, u32[]{:S(2)}, u32[]{:S(2)}) collective-permute-start(f32[8,8320]{1,0:T(8,128)} %pad_maximum_fusion.3), channel_id=1, source_target_pairs={{0,64},{8,72},{16,80},{24,88},{32,96},{40,104},{48,112},{56,120},{... | collective-permute-start | bytes 798728 | tf_op jit(solution)/shard_map/ppermute | solution.py:45
  279.0 11.0 %collective-permute-done.6 = f32[8,8320]{1,0:T(8,128)} collective-permute-done((f32[8,8320]{1,0:T(8,128)}, f32[8,8320]{1,0:T(8,128)}, u32[]{:S(2)}, u32[]{:S(2)}) %collective-permute-start.6) | collective-permute-done | bytes 266272 | tf_op jit(solution)/shard_map/ppermute | solution.py:45
  296.1 5.2 %collective-permute-done.7 = f32[8,8320]{1,0:T(8,128)} collective-permute-done((f32[8,8320]{1,0:T(8,128)}, f32[8,8320]{1,0:T(8,128)}, u32[]{:S(2)}, u32[]{:S(2)}) %collective-permute-start.7) | collective-permute-done | bytes 266272 | tf_op jit(solution)/shard_map/ppermute | solution.py:45
  304.4 10.2 %collective-permute-done.8 = f32[8,8192]{1,0:T(8,128)S(1)} collective-permute-done((f32[8,8192]{1,0:T(8,128)S(1)}, f32[8,8192]{1,0:T(8,128)S(1)}, u32[]{:S(2)}, u32[]{:S(2)}) %collective-permute-start.8) | collective-permute-done | bytes 262176 | tf_op jit(solution)/shard_map/ppermute | solution.py:40
  350.5 3.7 gather_fusion.1
  357.3 3.8 collective-permute-start.13
  363.1 3.8 gather_fusion
  376.0 4.9 %collective-permute-start.14 = (f32[256,2,256]{2,0,1:T(8,128)S(1)}, f32[256,2,256]{2,0,1:T(8,128)S(1)}, u32[]{:S(2)}, u32[]{:S(2)}) collective-permute-start(f32[256,2,256]{2,0,1:T(8,128)S(1)} %select_bitcast_fusion.2), channel_id=1, source_target_pairs={{0,2},{1,3},{2,0},{3,1},{4,6},{5,7},{6,4},{7,5},{8,10},{9,11},{10,... | collective-permute-start | bytes 1572872 | tf_op jit(solution)/shard_map/ppermute | solution.py:89
  380.9 13.5 %collective-permute-done.10 = f32[256,4,256]{2,0,1:T(8,128)} collective-permute-done((f32[256,4,256]{2,0,1:T(8,128)}, f32[256,4,256]{2,0,1:T(8,128)}, u32[]{:S(2)}, u32[]{:S(2)}) %collective-permute-start.10) | collective-permute-done | bytes 1048608 | tf_op jit(solution)/shard_map/ppermute | solution.py:89
  396.8 4.6 %collective-permute-start.11 = (f32[256,2,256]{2,0,1:T(8,128)}, f32[256,2,256]{2,0,1:T(8,128)}, u32[]{:S(2)}, u32[]{:S(2)}) collective-permute-start(f32[256,2,256]{2,0,1:T(8,128)} %select_bitcast_fusion.3), channel_id=1, source_target_pairs={{0,2},{1,3},{2,0},{3,1},{4,6},{5,7},{6,4},{7,5},{8,10},{9,11},{10,... | collective-permute-start | bytes 1572872 | tf_op jit(solution)/shard_map/ppermute | solution.py:89
  401.7 5.7 %collective-permute-start.15 = (f32[256,1,256]{2,0,1:T(8,128)S(1)}, f32[256,1,256]{2,0,1:T(8,128)S(1)}, u32[]{:S(2)}, u32[]{:S(2)}) collective-permute-start(f32[256,1,256]{2,0,1:T(8,128)S(1)} %select_bitcast_fusion.4), channel_id=1, source_target_pairs={{0,4},{1,5},{2,6},{3,7},{4,0},{5,1},{6,2},{7,3},{8,12},{9,13},{10,... | collective-permute-start | bytes 786440 | tf_op jit(solution)/shard_map/ppermute | solution.py:89
  407.4 7.8 %collective-permute-done.11 = f32[256,2,256]{2,0,1:T(8,128)} collective-permute-done((f32[256,2,256]{2,0,1:T(8,128)}, f32[256,2,256]{2,0,1:T(8,128)}, u32[]{:S(2)}, u32[]{:S(2)}) %collective-permute-start.11) | collective-permute-done | bytes 524320 | tf_op jit(solution)/shard_map/ppermute | solution.py:89
  416.4 5.7 %collective-permute-start.12 = (f32[256,1,256]{2,0,1:T(8,128)S(1)}, f32[256,1,256]{2,0,1:T(8,128)S(1)}, u32[]{:S(2)}, u32[]{:S(2)}) collective-permute-start(f32[256,1,256]{2,0,1:T(8,128)S(1)} %select_bitcast_fusion.6), channel_id=1, source_target_pairs={{0,4},{1,5},{2,6},{3,7},{4,0},{5,1},{6,2},{7,3},{8,12},{9,13},{10,... | collective-permute-start | bytes 786440 | tf_op jit(solution)/shard_map/ppermute | solution.py:89
  422.8 13.3 %collective-permute-done.12 = f32[256,1,256]{2,0,1:T(8,128)S(1)} collective-permute-done((f32[256,1,256]{2,0,1:T(8,128)S(1)}, f32[256,1,256]{2,0,1:T(8,128)S(1)}, u32[]{:S(2)}, u32[]{:S(2)}) %collective-permute-start.12) | collective-permute-done | bytes 262176 | tf_op jit(solution)/shard_map/ppermute | solution.py:89
  (235 shorter events, 112.8 us)
Async XLA Ops:
  5.1 14.7 %copy-start.26 = (bf16[256,256]{1,0:T(8,128)(2,1)S(1)}, bf16[256,256]{1,0:T(8,128)(2,1)}, u32[]{:S(2)}) copy-start(bf16[256,256]{1,0:T(8,128)(2,1)} %param.11) | copy-start | bytes 393220
  5.1 14.7 %copy-start.27 = (bf16[256,256]{1,0:T(8,128)(2,1)S(1)}, bf16[256,256]{1,0:T(8,128)(2,1)}, u32[]{:S(2)}) copy-start(bf16[256,256]{1,0:T(8,128)(2,1)} %param.19) | copy-start | bytes 393220
  5.1 189.8 %all-to-all-start = ((bf16[64,32,1288]{2,1,0:T(8,128)(2,1)}), bf16[64,32,1288]{2,1,0:T(8,128)(2,1)}, u32[]{:S(2)}, u32[]{:S(2)}) async-start(bf16[64,32,1288]{2,1,0:T(8,128)(2,1)} %stack.5), calls=%async_computation | async-start | bytes 11534336 | tf_op jit(solution)/shard_map/all_to_all | solution.py:207
  19.8 131.2 %collective-permute-start = (bf16[256,512]{1,0:T(8,128)(2,1)S(1)}, bf16[256,512]{1,0:T(8,128)(2,1)S(1)}, u32[]{:S(2)}, u32[]{:S(2)}) collective-permute-start(bf16[256,512]{1,0:T(8,128)(2,1)S(1)} %constant_dynamic-update-slice_fusion), channel_id=1, source_target_pairs={{0,4},{1,5},{2,6},{3,7},{4,0},{5,1},{6,2},{7,3},{8,12},{9,13},{10,... | collective-permute-start | bytes 786440 | tf_op jit(solution)/shard_map/ppermute | solution.py:184
  151.3 16.8 %collective-permute-start.1 = (bf16[512,512]{1,0:T(8,128)(2,1)S(1)}, bf16[512,512]{1,0:T(8,128)(2,1)S(1)}, u32[]{:S(2)}, u32[]{:S(2)}) collective-permute-start(bf16[512,512]{1,0:T(8,128)(2,1)S(1)} %maximum_select_fusion.2), channel_id=1, source_target_pairs={{0,2},{1,3},{2,0},{3,1},{4,6},{5,7},{6,4},{7,5},{8,10},{9,11},{10,... | collective-permute-start | bytes 1572872 | tf_op jit(solution)/shard_map/ppermute | solution.py:184
  168.6 25.6 %collective-permute-start.2 = (bf16[1024,512]{1,0:T(8,128)(2,1)S(1)}, bf16[1024,512]{1,0:T(8,128)(2,1)S(1)}, u32[]{:S(2)}, u32[]{:S(2)}) collective-permute-start(bf16[1024,512]{1,0:T(8,128)(2,1)S(1)} %maximum_select_fusion.1), channel_id=1, source_target_pairs={{0,1},{1,0},{2,3},{3,2},{4,5},{5,4},{6,7},{7,6},{8,9},{9,8},{10,11... | collective-permute-start | bytes 3145736 | tf_op jit(solution)/shard_map/ppermute | solution.py:184
  223.5 4.0 collective-permute-start.3
  228.8 65.8 %copy-start.41 = (s32[8]{0:T(128)S(1)}, s32[8]{0:T(128)}, u32[]{:S(2)}) copy-start(s32[8]{0:T(128)} %constant.154) | copy-start | bytes 100
  228.8 12.5 %collective-permute-start.4 = (f32[8,8320]{1,0:T(8,128)}, f32[8,8320]{1,0:T(8,128)}, u32[]{:S(2)}, u32[]{:S(2)}) collective-permute-start(f32[8,8320]{1,0:T(8,128)} %pad_maximum_fusion.1), channel_id=1, source_target_pairs={{0,16},{8,24},{16,0},{24,8},{32,48},{40,56},{48,32},{56,40},{64,80... | collective-permute-start | bytes 798728 | tf_op jit(solution)/shard_map/ppermute | solution.py:45
  242.0 53.2 %copy-start.40 = (f32[8]{0:T(128)S(1)}, f32[8]{0:T(128)}, u32[]{:S(2)}) copy-start(f32[8]{0:T(128)} %param.17) | copy-start | bytes 100
  242.0 53.9 %copy-start.14 = (bf16[256,256]{0,1:T(8,128)(2,1)S(1)}, bf16[256,256]{0,1:T(8,128)(2,1)}, u32[]{:S(2)}) copy-start(bf16[256,256]{0,1:T(8,128)(2,1)} %copy-done.13) | copy-start | bytes 393220
  243.9 20.1 %collective-permute-start.5 = (f32[8,8320]{1,0:T(8,128)}, f32[8,8320]{1,0:T(8,128)}, u32[]{:S(2)}, u32[]{:S(2)}) collective-permute-start(f32[8,8320]{1,0:T(8,128)} %pad_maximum_fusion.2), channel_id=1, source_target_pairs={{0,32},{8,40},{16,48},{24,56},{32,0},{40,8},{48,16},{56,24},{64,96... | collective-permute-start | bytes 798728 | tf_op jit(solution)/shard_map/ppermute | solution.py:45
  266.6 23.4 %collective-permute-start.6 = (f32[8,8320]{1,0:T(8,128)}, f32[8,8320]{1,0:T(8,128)}, u32[]{:S(2)}, u32[]{:S(2)}) collective-permute-start(f32[8,8320]{1,0:T(8,128)} %pad_maximum_fusion.3), channel_id=1, source_target_pairs={{0,64},{8,72},{16,80},{24,88},{32,96},{40,104},{48,112},{56,120},{... | collective-permute-start | bytes 798728 | tf_op jit(solution)/shard_map/ppermute | solution.py:45
  290.8 27.4 %copy-start.25 = (f32[8,2,128]{2,0,1:T(8,128)S(1)}, f32[8,2,128]{2,0,1:T(8,128)}, u32[]{:S(2)}) copy-start(f32[8,2,128]{2,0,1:T(8,128)} %copy-done.24) | copy-start | bytes 24580
  292.7 8.6 %collective-permute-start.7 = (f32[8,8320]{1,0:T(8,128)}, f32[8,8320]{1,0:T(8,128)}, u32[]{:S(2)}, u32[]{:S(2)}) collective-permute-start(f32[8,8320]{1,0:T(8,128)} %pad_maximum_fusion.4), channel_id=1, source_target_pairs={{0,128},{8,136},{16,144},{24,152},{32,160},{40,168},{48,176},{56,1... | collective-permute-start | bytes 798728 | tf_op jit(solution)/shard_map/ppermute | solution.py:45
  303.1 11.5 %collective-permute-start.8 = (f32[8,8192]{1,0:T(8,128)S(1)}, f32[8,8192]{1,0:T(8,128)S(1)}, u32[]{:S(2)}, u32[]{:S(2)}) collective-permute-start(f32[8,8192]{1,0:T(8,128)S(1)} %add_select_fusion.4), channel_id=1, source_target_pairs={{0,256},{16,272},{32,288},{48,304},{64,320},{80,336},{96,352},{112... | collective-permute-start | bytes 786440 | tf_op jit(solution)/shard_map/ppermute | solution.py:40
  316.0 7.7 %collective-permute-start.9 = (f32[8,8192]{1,0:T(8,128)S(1)}, f32[8,8192]{1,0:T(8,128)S(1)}, u32[]{:S(2)}, u32[]{:S(2)}) collective-permute-start(f32[8,8192]{1,0:T(8,128)S(1)} %add_select_fusion), channel_id=1, source_target_pairs={{0,8},{8,0},{16,24},{24,16},{32,40},{40,32},{48,56},{56,48},{64,72... | collective-permute-start | bytes 786440 | tf_op jit(solution)/shard_map/ppermute | solution.py:54
  357.3 17.1 %collective-permute-start.13 = (f32[256,4,256]{2,0,1:T(8,128)S(1)}, f32[256,4,256]{2,0,1:T(8,128)}, u32[]{:S(2)}, u32[]{:S(2)}) collective-permute-start(f32[256,4,256]{2,0,1:T(8,128)S(1)} %select_bitcast_fusion), channel_id=1, source_target_pairs={{0,1},{1,0},{2,3},{3,2},{4,5},{5,4},{6,7},{7,6},{8,11},{9,10},{10,... | collective-permute-start | bytes 3145736 | tf_op jit(solution)/shard_map/ppermute | solution.py:89
  371.9 22.6 %collective-permute-start.10 = (f32[256,4,256]{2,0,1:T(8,128)}, f32[256,4,256]{2,0,1:T(8,128)}, u32[]{:S(2)}, u32[]{:S(2)}) collective-permute-start(f32[256,4,256]{2,0,1:T(8,128)} %select_bitcast_fusion.1), channel_id=1, source_target_pairs={{0,1},{1,0},{2,3},{3,2},{4,5},{5,4},{6,7},{7,6},{8,11},{9,10},{10,... | collective-permute-start | bytes 3145736 | tf_op jit(solution)/shard_map/ppermute | solution.py:89
  374.3 20.2 %copy-start.1 = (f32[256,8,256]{2,0,1:T(8,128)S(1)}, f32[256,8,256]{2,0,1:T(8,128)}, u32[]{:S(2)}) copy-start(f32[256,8,256]{2,0,1:T(8,128)} %copy-done) | copy-start | bytes 6291460
  376.0 25.6 %collective-permute-start.14 = (f32[256,2,256]{2,0,1:T(8,128)S(1)}, f32[256,2,256]{2,0,1:T(8,128)S(1)}, u32[]{:S(2)}, u32[]{:S(2)}) collective-permute-start(f32[256,2,256]{2,0,1:T(8,128)S(1)} %select_bitcast_fusion.2), channel_id=1, source_target_pairs={{0,2},{1,3},{2,0},{3,1},{4,6},{5,7},{6,4},{7,5},{8,10},{9,11},{10,... | collective-permute-start | bytes 1572872 | tf_op jit(solution)/shard_map/ppermute | solution.py:89
  396.8 18.4 %collective-permute-start.11 = (f32[256,2,256]{2,0,1:T(8,128)}, f32[256,2,256]{2,0,1:T(8,128)}, u32[]{:S(2)}, u32[]{:S(2)}) collective-permute-start(f32[256,2,256]{2,0,1:T(8,128)} %select_bitcast_fusion.3), channel_id=1, source_target_pairs={{0,2},{1,3},{2,0},{3,1},{4,6},{5,7},{6,4},{7,5},{8,10},{9,11},{10,... | collective-permute-start | bytes 1572872 | tf_op jit(solution)/shard_map/ppermute | solution.py:89
  401.7 20.4 %collective-permute-start.15 = (f32[256,1,256]{2,0,1:T(8,128)S(1)}, f32[256,1,256]{2,0,1:T(8,128)S(1)}, u32[]{:S(2)}, u32[]{:S(2)}) collective-permute-start(f32[256,1,256]{2,0,1:T(8,128)S(1)} %select_bitcast_fusion.4), channel_id=1, source_target_pairs={{0,4},{1,5},{2,6},{3,7},{4,0},{5,1},{6,2},{7,3},{8,12},{9,13},{10,... | collective-permute-start | bytes 786440 | tf_op jit(solution)/shard_map/ppermute | solution.py:89
  416.4 19.7 %collective-permute-start.12 = (f32[256,1,256]{2,0,1:T(8,128)S(1)}, f32[256,1,256]{2,0,1:T(8,128)S(1)}, u32[]{:S(2)}, u32[]{:S(2)}) collective-permute-start(f32[256,1,256]{2,0,1:T(8,128)S(1)} %select_bitcast_fusion.6), channel_id=1, source_target_pairs={{0,4},{1,5},{2,6},{3,7},{4,0},{5,1},{6,2},{7,3},{8,12},{9,13},{10,... | collective-permute-start | bytes 786440 | tf_op jit(solution)/shard_map/ppermute | solution.py:89
  (35 other events, 120.4 us)
